TPU v7x, 32 devices: a whole 2x2x4 slice. The times are simulated.
32 devices in a mesh: seq: 8 (over y, x, core), head: 4 (over z).
Axes of the slice: x: 2, y: 2, z: 4, core: 2. Of those that a mesh axis runs over, the one named last changes fastest.
Arguments:
- tokens: bfloat16 [8192, 1024], P(('seq', 'head')), may hold values from -6 to 6
- qkv_weight: bfloat16 [1024, 3, 1024], P(None, None, 'head'), may hold values from -0.1875 to 0.1875
- out_weight: bfloat16 [1024, 1024], P('head'), may hold values from -0.1875 to 0.1875
- up_weight: bfloat16 [1024, 2, 2816], P(None, None, 'head'), may hold values from -0.1875 to 0.1875
- down_weight: bfloat16 [2816, 1024], P('head'), may hold values from -0.109375 to 0.109375
- vocab_weight: bfloat16 [1024, 16384], P(None, 'head'), may hold values from -0.1875 to 0.1875
- persistent: bfloat16 [2, 16, 1024], P(None, None, 'head'), may hold values from -120 to 120
- norm_gains: float32 [3, 1024], replicated, may hold values from 0.5 to 1.5
- write_rate: float32 [8192, 8], P('seq', 'head'), may hold values from 0.02 to 0.2
- forget: float32 [128, 8], P('seq', 'head'), may hold values from 0 to 1
- momentum: float32 [128, 8], P('seq', 'head'), may hold values from 0.2 to 0.9
- prompt_spans: int32 [4], replicated, may hold values from 1 to 64, as said below
Outputs:
- logit_max: float32 [8192], P('seq')
- state_rms: float32 [4, 8], P(None, 'head')
Inputs may be any that keep to these rules, and one draw needn't show every extreme that they name: Prompt p holds prompt_spans[p] consecutive spans of 64 tokens, the prompts packed in order from token 0; they sum to 128, and prompt 1 is the longest, with exactly 64 spans.
All inputs are finite; a program needn't handle non-finite values.
Results may differ from a plain program's by a relative error of at most 0.0047.
Values may be sent and summed in bfloat16 or wider, within the bound.
No kernel may reach another device: no remote copies, remote signals or barrier semaphores. Data moves between devices by JAX's collectives and lax.ppermute only.
A program may use at most 128 MiB of HBM per device.

v0:
```python
import jax
import jax.numpy as jnp
from jax import lax
from jax.sharding import PartitionSpec as P

D = 1024
HS = 128
NPER = 16
SEG = 1024
CH = 64
SEQS = 4
eps_norm = 1e-05
eps_unit = 1e-06
score_scale = 10.0
masked_score = -1e30


def passed_along(array, axis, by):
    size = lax.axis_size(axis)
    pairs = [(i, i + by) for i in range(size) if 0 <= i + by < size]
    return lax.ppermute(array, axis, pairs)


def carried_in(part, axis, combine, identity):
    place = lax.axis_index(axis)
    gathered = jax.tree.map(lambda a: lax.all_gather(a, axis), part)
    state = jax.tree.map(lambda a, e: jnp.zeros_like(a) + jnp.asarray(e, a.dtype), part, identity)

    def one(step, state):
        return combine(
            state, jax.tree.map(lambda a: lax.dynamic_index_in_dim(a, step, 0, False), gathered)
        )

    return lax.fori_loop(0, place, one, state)


def rms_scale(values, gain):
    return values * lax.rsqrt(jnp.mean(values * values, axis=-1, keepdims=True) + eps_norm) * gain


def unit_rows(values):
    widened = values.astype(jnp.float32)
    return (
        widened * lax.rsqrt(jnp.sum(widened * widened, axis=-1, keepdims=True) + eps_unit)
    ).astype(jnp.bfloat16)


def segment_starts(positions, prompt_spans):
    prompt_ends = jnp.cumsum(prompt_spans)
    first_tokens = (prompt_ends - prompt_spans) * CH
    reached = positions[:, None] >= first_tokens[None, :]
    prompt_first = jnp.max(jnp.where(reached, first_tokens[None, :], 0), axis=1)
    return prompt_first + (positions - prompt_first) // SEG * SEG


def compose(later, earlier):
    return jnp.stack(
        [
            later[..., 0] * earlier[..., 0],
            later[..., 0] * earlier[..., 1] + later[..., 1] * earlier[..., 2],
            later[..., 2] * earlier[..., 2],
        ],
        axis=-1,
    )


def apply_map(coeffs, memory, moment):
    moved_memory = coeffs[:, 0, None, None] * memory + coeffs[:, 1, None, None] * moment
    return (moved_memory, coeffs[:, 2, None, None] * moment)


def chain_combine(earlier, later):
    moved_memory, moved_moment = apply_map(later[0], earlier[1], earlier[2])
    return (compose(later[0], earlier[0]), moved_memory + later[1], moved_moment + later[2])


def to_owners(local_rows, project):
    return project(lax.all_gather(local_rows, "head", axis=0, tiled=True), jnp.int32(0))


def from_owners(term, share_rows):
    return lax.psum_scatter(
        term(jnp.int32(0), share_rows * lax.axis_size("head")),
        "head",
        scatter_dimension=0,
        tiled=True,
    )


def local(
    tokens,
    qkv_weight,
    out_weight,
    up_weight,
    down_weight,
    vocab_weight,
    persistent,
    norm_gains,
    write_rate,
    forget,
    momentum,
    prompt_spans,
):
    share_rows = tokens.shape[0]
    head_count = lax.axis_size("head")
    seq_count = lax.axis_size("seq")
    block_rows = share_rows * head_count
    heads_here = write_rate.shape[1]
    current_width = heads_here * HS
    seq_index = lax.axis_index("seq")
    head_index = lax.axis_index("head")
    qkv_matrix = qkv_weight.reshape(D, 3 * current_width)
    highest = lax.Precision.HIGHEST

    def token_project(piece, start):
        normed = rms_scale(piece.astype(jnp.float32), norm_gains[0]).astype(jnp.bfloat16)
        projected = jnp.dot(normed, qkv_matrix, preferred_element_type=jnp.float32).astype(
            jnp.bfloat16
        )
        return projected

    gathered = to_owners(tokens, token_project)
    out_full = lax.all_gather(
        out_weight + (gathered[0, 0] * 0).astype(out_weight.dtype), "head", axis=0, tiled=True
    )
    down_full = lax.all_gather(
        down_weight + (gathered[0, 1] * 0).astype(down_weight.dtype), "head", axis=0, tiled=True
    )
    projected = gathered
    query_unit = unit_rows(projected[:, :current_width].reshape(block_rows, heads_here, HS))
    key_unit = unit_rows(
        projected[:, current_width : 2 * current_width].reshape(block_rows, heads_here, HS)
    )
    value_rows = projected[:, 2 * current_width :].reshape(block_rows, heads_here, HS)
    reach = SEG // block_rows
    moved_keys, moved_values = passed_along((key_unit, value_rows), "seq", 1)
    earlier_keys = [moved_keys]
    earlier_values = [moved_values]
    all_keys = jnp.concatenate(earlier_keys + [key_unit], axis=0)
    all_values = jnp.concatenate(earlier_values + [value_rows], axis=0)
    first_row = seq_index * block_rows
    query_positions = first_row + jnp.arange(block_rows, dtype=jnp.int32)
    key_positions = (
        first_row - reach * block_rows + jnp.arange((reach + 1) * block_rows, dtype=jnp.int32)
    )
    query_segments = segment_starts(query_positions, prompt_spans)
    key_segments = segment_starts(key_positions, prompt_spans)
    allowed = (
        (key_segments[None, :] == query_segments[:, None])
        & (key_positions[None, :] <= query_positions[:, None])
        & (key_positions[None, :] >= 0)
    )
    persist_keys = persistent[0].reshape(NPER, heads_here, HS)
    persist_values = persistent[1].reshape(NPER, heads_here, HS)
    scores = score_scale * jnp.einsum(
        "qhd,khd->hqk", query_unit, all_keys, preferred_element_type=jnp.float32
    )
    scores = jnp.where(allowed[None], scores, masked_score)
    extra = score_scale * jnp.einsum(
        "qhd,phd->hqp", query_unit, persist_keys, preferred_element_type=jnp.float32
    )
    top = jnp.maximum(jnp.max(scores, axis=-1), jnp.max(extra, axis=-1))[..., None]
    near = jnp.where(allowed[None], jnp.exp(scores - top), 0.0)
    far = jnp.exp(extra - top)
    total = jnp.sum(near, axis=-1, keepdims=True) + jnp.sum(far, axis=-1, keepdims=True)
    near_weights = (near / total).astype(jnp.bfloat16)
    far_weights = (far / total).astype(jnp.bfloat16)
    attended = jnp.einsum(
        "hqk,khd->qhd", near_weights, all_values, preferred_element_type=jnp.float32
    )
    attended = attended + jnp.einsum(
        "hqp,phd->qhd", far_weights, persist_values, preferred_element_type=jnp.float32
    )
    total_spans = block_rows // CH
    span_queries = query_unit.reshape(total_spans, CH, heads_here, HS)
    span_keys = key_unit.reshape(total_spans, CH, heads_here, HS)
    span_values = value_rows.reshape(total_spans, CH, heads_here, HS)
    span_rates = write_rate.reshape(total_spans, CH, heads_here)
    prompt_ends = jnp.cumsum(prompt_spans)
    first_spans = prompt_ends - prompt_spans
    span_ids = seq_index * total_spans + jnp.arange(total_spans, dtype=jnp.int32)
    keep = jnp.where(jnp.any(span_ids[:, None] == first_spans[None, :], axis=1), 0.0, 1.0).astype(
        jnp.float32
    )
    causal = (jnp.arange(CH)[:, None] >= jnp.arange(CH)[None, :]).astype(jnp.float32)
    values_wide = span_values.astype(jnp.float32)
    written = jnp.einsum(
        "cthi,cthj->chij",
        span_rates[..., None] * values_wide,
        span_keys.astype(jnp.float32),
        precision=highest,
    )
    affinity = jnp.einsum(
        "cthd,cshd->chts", span_queries, span_keys, preferred_element_type=jnp.float32
    )
    affinity = affinity * causal[None, None] * jnp.transpose(span_rates, (0, 2, 1))[:, :, None, :]
    local_recall = jnp.einsum("chts,cshi->cthi", affinity, values_wide, precision=highest)
    decay_memory = forget * keep[:, None]
    decay_moment = momentum * keep[:, None]
    identity_coeffs = jnp.tile(jnp.array([1.0, 0.0, 1.0], jnp.float32), (heads_here, 1))
    zero_state = jnp.zeros((heads_here, HS, HS), jnp.float32)

    def advance(carry, inputs):
        coeffs, memory, moment = carry
        current_written, memory_rate, moment_rate = inputs
        step_coeffs = jnp.stack([memory_rate, moment_rate, moment_rate], axis=-1)
        next_moment = moment_rate[:, None, None] * moment + current_written
        next_memory = (
            memory_rate[:, None, None] * memory
            + moment_rate[:, None, None] * moment
            + current_written
        )
        return ((compose(step_coeffs, coeffs), next_memory, next_moment), (coeffs, memory))

    (last_coeffs, last_memory, last_moment), (coeffs_before, memory_before) = lax.scan(
        advance, (identity_coeffs, zero_state, zero_state), (written, decay_memory, decay_moment)
    )
    _, incoming_memory, incoming_moment = carried_in(
        (last_coeffs, last_memory, last_moment),
        "seq",
        chain_combine,
        (identity_coeffs, zero_state, zero_state),
    )
    true_before = (
        memory_before
        + coeffs_before[..., 0, None, None] * incoming_memory[None]
        + coeffs_before[..., 1, None, None] * incoming_moment[None]
    )
    recalled = local_recall + jnp.einsum(
        "chij,cthj->cthi",
        true_before * keep[:, None, None, None],
        span_queries.astype(jnp.float32),
        precision=highest,
    )
    memory_after = jnp.concatenate([memory_before[1:], last_memory[None]], axis=0)
    coeffs_after = jnp.concatenate([coeffs_before[1:], last_coeffs[None]], axis=0)
    true_after = (
        memory_after
        + coeffs_after[..., 0, None, None] * incoming_memory[None]
        + coeffs_after[..., 1, None, None] * incoming_moment[None]
    )
    spread = jnp.sqrt(jnp.mean(true_after * true_after, axis=(2, 3)))
    hit_spans = span_ids[None, :] == (prompt_ends - 1)[:, None]
    state_slots = jnp.sum(jnp.where(hit_spans[:, :, None], spread[None], 0.0), axis=1)
    mixed = (
        (attended + recalled.reshape(block_rows, heads_here, HS))
        .astype(jnp.bfloat16)
        .reshape(block_rows, current_width)
    )
    ff_here = down_weight.shape[0]
    gate_up = up_weight.reshape(D, 2 * ff_here)

    def ffn_hidden(normed_rows):
        gated = jnp.dot(normed_rows, gate_up, preferred_element_type=jnp.float32)
        return (jax.nn.silu(gated[:, :ff_here]) * gated[:, ff_here:]).astype(jnp.bfloat16)

    def ffn_project(piece, start):
        return ffn_hidden(piece)

    pieces = mixed.reshape(head_count, share_rows, current_width)
    swapped = lax.all_to_all(pieces, "head", 0, 0, tiled=False)
    mixed_rows = jnp.transpose(swapped, (1, 0, 2)).reshape(share_rows, head_count * current_width)
    residual = tokens.astype(jnp.float32) + jnp.dot(
        mixed_rows, out_full, preferred_element_type=jnp.float32
    )
    residual = residual + (down_full[0, 0] * 0).astype(jnp.float32)
    hidden = to_owners(rms_scale(residual, norm_gains[1]).astype(jnp.bfloat16), ffn_project)
    hidden_pieces = hidden.reshape(head_count, share_rows, ff_here)
    hidden_swapped = lax.all_to_all(hidden_pieces, "head", 0, 0, tiled=False)
    hidden_rows = jnp.transpose(hidden_swapped, (1, 0, 2)).reshape(share_rows, head_count * ff_here)
    second = residual + jnp.dot(hidden_rows, down_full, preferred_element_type=jnp.float32)
    final = rms_scale(second, norm_gains[2]).astype(jnp.bfloat16)

    def vocab_maxima(piece, start):
        return jnp.max(jnp.dot(piece, vocab_weight, preferred_element_type=jnp.float32), axis=1)

    row_maxima = to_owners(final, vocab_maxima)
    logit_max = lax.pmax(row_maxima, "head")
    state_rms = jnp.sum(lax.all_gather(state_slots, "seq"), axis=0)
    return (logit_max, state_rms)


def solution(mesh):
    in_specs = (
        P(("seq", "head"), None),
        P(None, None, "head"),
        P("head", None),
        P(None, None, "head"),
        P("head", None),
        P(None, "head"),
        P(None, None, "head"),
        P(),
        P("seq", "head"),
        P("seq", "head"),
        P("seq", "head"),
        P(),
    )
    out_specs = (P("seq"), P(None, "head"))
    return jax.shard_map(local, mesh=mesh, in_specs=in_specs, out_specs=out_specs, check_vma=False)
```

profile of v0, /device:TPU:0, one launch (start us, length us, event | category | flops | bytes accessed | tf_op | source)
XLA Modules:
  0.0 514.6 jit_solution(8284672369578851746)
XLA Ops:
  8.1 2.7 copy.217
  13.5 44.8 %all-gather.14.cloned.1.call-done = bf16[1024,1024]{1,0:T(8,128)(2,1)} async-done(((bf16[256,1024]{1,0:T(8,128)(2,1)}), bf16[1024,1024]{1,0:T(8,128)(2,1)}) %all-gather.14.cloned.1.call-update) | async-done | bytes 2097168 | tf_op jit(solution)/shard_map/all_gather | solution.py:78
  60.6 3.3 fusion.23
  70.6 2.8 reshape.366
  73.4 3.5 copy.229
  77.0 3.1 convert_multiply_fusion.2
  80.1 3.5 fusion.43
  83.7 37.7 %while.34 = (s32[]{:T(128)}, f32[2,3]{0,1:T(4,128)S(1)}, f32[2,128,128]{2,1,0:T(8,128)S(1)}, f32[2,128,128]{2,1,0:T(8,128)S(1)}, f32[16,2,3]{2,1,0:T(2,128)}, /*...) while((s32[]{:T(128)}, f32[2,3]{0,1:T(4,128)S(1)}, ...), condition=%wide.region_12.13_spmd.clone, body=%wide.region_11.12_spmd.clone.sunk | while | flops 262167 | bytes 919916 | solution.py:215
  130.2 6.4 %and_and_fusion = pred[1024,2048]{1,0:T(8,128)(4,1)} fusion(s32[2048]{0:T(1024)S(1)} %iota_add_fusion, s32[2048]{0:T(1024)S(1)} %fusion.57, s32[1024]{0:T(1024)S(1)} %iota_add_fusion.1, s32[1024]{0:T(1024)S(1)} %fusion.64, pred[2048]{0:T(1024)(128)(4,1)S(1)} %fusion.61), kind=kLoop, calls=%fused_computation.25 | loop fusion | flops 8388608 | bytes 2123776 | tf_op jit(solution)/shard_map/and | solution.py:149
  136.7 9.0 %all-gather.4 = f32[8,2,3]{2,1,0:T(2,128)} all-gather(f32[1,2,3]{2,1,0:T(2,128)S(1)} %bitcast.132), channel_id=2, replica_groups=mesh['seq'=8,'head'=4] {'seq'}, dimensions={0}, use_global_device_ids=true | all-gather | bytes 216 | tf_op jit(solution)/shard_map/all_gather | solution.py:26
  149.8 3.5 collective-permute-start.1
  153.3 2.9 reshape.365
  160.3 3.5 copy.226
  164.6 4.1 collective-permute-start
  173.2 3.3 fusion.30
  176.5 4.9 fusion.3
  181.5 5.6 %fusion.4 = f32[2,1024]{1,0:T(2,128)S(1)} fusion(f32[2,1024,2048]{2,1,0:T(8,128)S(1)} %get-tuple-element.215, f32[2,1024]{1,0:T(2,128)S(1)} %max.9, pred[1024,2048]{1,0:T(8,128)(4,1)S(1)} %copy-done.5), kind=kLoop, calls=%fused_computation.24 | loop fusion | flops 20969472 | bytes 18890752 | tf_op jit(solution)/shard_map/reduce_sum | solution.py:165
  189.7 4.3 fusion.27
  198.4 11.1 %fusion.35 = bf16[1024,2,128]{0,2,1:T(8,128)(2,1)} fusion(f32[1024,2,128]{0,2,1:T(8,128)} %copy.242, f32[1024,2,128]{0,2,1:T(8,128)} %convolution_bitcast_fusion, f32[2,1024,2048]{2,1,0:T(8,128)} %copy-done.3, f32[2,1024]{1,0:T(2,128)S(1)} %add.232, f32[2,1024]{1,0:T(2,128)S(1)} %max.9, pred[1024,2048]{1,0:T(8,128)(4,1)} %and_and_fusion, ...), kind=kOutput, calls=%fused_computation.61 | convolution fusion | flops 1101791232 | bytes 22560768 | tf_op jit(solution)/shard_map/hqk,khd->qhd/dot_general | solution.py:168
  213.7 4.1 all-to-all-start
  217.9 72.7 %all-gather.18.cloned.1.call-done = bf16[2816,1024]{1,0:T(8,128)(2,1)} async-done(((bf16[704,1024]{1,0:T(8,128)(2,1)}), bf16[2816,1024]{1,0:T(8,128)(2,1)}) %all-gather.18.cloned.1.call-update) | async-done | bytes 5767184 | tf_op jit(solution)/shard_map/all_gather | solution.py:126
  292.5 43.8 %all-gather.16.cloned.1.call-done = bf16[1024,1024]{1,0:T(8,128)(2,1)} async-done(((bf16[256,1024]{1,0:T(8,128)(2,1)}), bf16[1024,1024]{1,0:T(8,128)(2,1)}) %all-gather.16.cloned.1.call-update) | async-done | bytes 2097168 | tf_op jit(solution)/shard_map/all_gather | solution.py:123
  336.3 2.7 multiply_reduce_fusion.1
  341.0 44.8 %all-gather.20.cloned.1.call-done = bf16[1024,1024]{1,0:T(8,128)(2,1)} async-done(((bf16[256,1024]{1,0:T(8,128)(2,1)}), bf16[1024,1024]{1,0:T(8,128)(2,1)}) %all-gather.20.cloned.1.call-update) | async-done | bytes 2097168 | tf_op jit(solution)/shard_map/all_gather | solution.py:78
  385.8 5.0 fusion.77
  395.7 38.3 %all_to_all.10 = bf16[4,256,704]{1,2,0:T(8,128)(2,1)S(1)} all-to-all(bf16[4,256,704]{1,2,0:T(8,128)(2,1)} %copy.245), channel_id=1, replica_groups=mesh['seq'=8,'head'=4] {'head'}, dimensions={0} | all-to-all | bytes 2883584 | tf_op jit(solution)/shard_map/all_to_all | solution.py:269
  434.0 4.4 multiply_reduce_fusion
  439.8 3.0 slice.102
  445.4 8.9 %all-gather.5 = f32[8,4,2]{1,2,0:T(2,128)S(1)} all-gather(f32[1,4,2]{1,2,0:T(2,128)S(1)} %bitcast.136), channel_id=5, replica_groups=mesh['seq'=8,'head'=4] {'seq'}, dimensions={0}, use_global_device_ids=true | all-gather | bytes 288 | tf_op jit(solution)/shard_map/all_gather | solution.py:279
  454.9 29.7 %all-gather.22.cloned.1.call-done = bf16[1024,1024]{1,0:T(8,128)(2,1)} async-done(((bf16[256,1024]{1,0:T(8,128)(2,1)}), bf16[1024,1024]{1,0:T(8,128)(2,1)}) %all-gather.22.cloned.1.call-update) | async-done | bytes 2097168 | tf_op jit(solution)/shard_map/all_gather | solution.py:78
  484.6 12.9 %convolution_reduce_fusion = f32[1024]{0:T(1024)S(1)} fusion(bf16[1024,1024]{1,0:T(8,128)(2,1)} %all-gather.22.cloned.1.call-done, bf16[1024,4096]{1,0:T(8,128)(2,1)} %param.22), kind=kOutput, calls=%fused_computation.32 | convolution fusion | flops 8594127872 | bytes 10489856 | tf_op jit(solution)/shard_map/dot_general | solution.py:275
  497.5 10.1 %pmax.7 = f32[1024]{0:T(1024)} all-reduce(f32[1024]{0:T(1024)S(1)} %convolution_reduce_fusion), channel_id=1, replica_groups=mesh['seq'=8,'head'=4] {'head'}, use_global_device_ids=true, to_apply=%region_18.19 | all-reduce | flops 1024 | bytes 8192 | tf_op jit(solution)/shard_map/pmax | solution.py:278
  (297 shorter events, 94.9 us)
Async XLA Ops:
  7.2 378.6 %copy-start = (bf16[1024,2,704]{0,2,1:T(8,128)(2,1)S(1)}, bf16[1024,2,704]{0,2,1:T(8,128)(2,1)}, u32[]{:S(2)}) copy-start(bf16[1024,2,704]{0,2,1:T(8,128)(2,1)} %param.20) | copy-start | bytes 8650756
  7.2 4.7 copy-start.36
  7.2 4.8 copy-start.34
  7.2 4.9 copy-start.35
  7.2 5.6 %copy-start.28 = (f32[3,1024]{1,0:T(4,128)S(1)}, f32[3,1024]{1,0:T(4,128)}, u32[]{:S(2)}) copy-start(f32[3,1024]{1,0:T(4,128)} %param.24) | copy-start | bytes 36868
  7.2 51.1 %all-gather.14.cloned.1.call-start = ((), (), s32[]{:S(2)}) async-start(), calls=%async_computation.2 | async-start | bytes 2621440 | tf_op jit(solution)/shard_map/all_gather | solution.py:78
  8.0 181.0 %all-gather.24.cloned.1.call-start = ((), (), s32[]{:S(2)}) async-start(), calls=%async_computation.7 | async-start | bytes 1179648 | tf_op jit(solution)/shard_map/all_gather | solution.py:26
  76.9 6.7 %copy-start.17 = (f32[1024,2]{0,1:T(2,128)}, f32[1024,2]{0,1:T(2,128)S(1)}, u32[]{:S(2)}) copy-start(f32[1024,2]{0,1:T(2,128)S(1)} %add_rsqrt_fusion) | copy-start | bytes 24580
  122.0 66.9 %all-gather.26.cloned.1.call-start = ((), (), s32[]{:S(2)}) async-start(), calls=%async_computation.8 | async-start | bytes 1179648 | tf_op jit(solution)/shard_map/all_gather | solution.py:26
  122.7 167.9 %all-gather.18.cloned.1.call-start = ((), (), s32[]{:S(2)}) async-start(), calls=%async_computation.4 | async-start | bytes 7208960 | tf_op jit(solution)/shard_map/all_gather | solution.py:126
  127.5 208.8 %all-gather.16.cloned.1.call-start = ((), (), s32[]{:S(2)}) async-start(), calls=%async_computation.3 | async-start | bytes 2621440 | tf_op jit(solution)/shard_map/all_gather | solution.py:123
  130.2 18.0 %copy-start.18 = (f32[1024,2]{0,1:T(2,128)S(1)}, f32[1024,2]{0,1:T(2,128)}, u32[]{:S(2)}) copy-start(f32[1024,2]{0,1:T(2,128)} %copy-done.17) | copy-start | bytes 24580
  136.7 16.5 %copy-start.29 = (f32[2,3]{1,0:T(2,128)}, f32[2,3]{1,0:T(2,128)S(1)}, u32[]{:S(2)}) copy-start(f32[2,3]{1,0:T(2,128)S(1)} %copy.238) | copy-start | bytes 76
  149.8 26.7 %collective-permute-start.1 = (bf16[1024,2,128]{2,0,1:T(8,128)(2,1)S(1)}, bf16[1024,2,128]{2,0,1:T(8,128)(2,1)}, u32[]{:S(2)}, u32[]{:S(2)}) collective-permute-start(bf16[1024,2,128]{2,0,1:T(8,128)(2,1)S(1)} %multiply_convert_fusion.4), channel_id=1, source_target_pairs={{0,4},{4,8},{8,12},{12,16},{16,20},{20,24},{24,28},{1,5},{5,9},{9,... | collective-permute-start | bytes 1572872 | tf_op jit(solution)/shard_map/ppermute | solution.py:21
  153.2 5.5 %copy-start.15 = (f32[16,2,3]{2,1,0:T(2,128)S(1)}, f32[16,2,3]{2,1,0:T(2,128)}, u32[]{:S(2)}) copy-start(f32[16,2,3]{2,1,0:T(2,128)} %get-tuple-element.113) | copy-start | bytes 1156
  158.7 5.1 copy-start.21
  163.8 7.4 %copy-start.19 = (f32[1024,2]{0,1:T(2,128)}, f32[1024,2]{0,1:T(2,128)S(1)}, u32[]{:S(2)}) copy-start(f32[1024,2]{0,1:T(2,128)S(1)} %add_rsqrt_fusion.1) | copy-start | bytes 24580
  164.6 33.8 %collective-permute-start = (bf16[1024,2,128]{0,2,1:T(8,128)(2,1)}, bf16[1024,2,128]{0,2,1:T(8,128)(2,1)}, u32[]{:S(2)}, u32[]{:S(2)}) collective-permute-start(bf16[1024,2,128]{0,2,1:T(8,128)(2,1)} %bitcast.5), channel_id=1, source_target_pairs={{0,4},{4,8},{8,12},{12,16},{16,20},{20,24},{24,28},{1,5},{5,9},{9,... | collective-permute-start | bytes 1572872 | tf_op jit(solution)/shard_map/ppermute | solution.py:21
  171.3 5.2 %copy-start.5 = (pred[1024,2048]{1,0:T(8,128)(4,1)S(1)}, pred[1024,2048]{1,0:T(8,128)(4,1)}, u32[]{:S(2)}) copy-start(pred[1024,2048]{1,0:T(8,128)(4,1)} %and_and_fusion) | copy-start | bytes 6291460
  171.3 5.2 %copy-start.12 = (f32[1024,2,128]{2,0,1:T(8,128)S(1)}, f32[1024,2,128]{2,0,1:T(8,128)}, u32[]{:S(2)}) copy-start(f32[1024,2,128]{2,0,1:T(8,128)} %copy.218) | copy-start | bytes 3145732
  171.3 5.2 %copy-start.20 = (f32[1024,2]{0,1:T(2,128)S(1)}, f32[1024,2]{0,1:T(2,128)}, u32[]{:S(2)}) copy-start(f32[1024,2]{0,1:T(2,128)} %copy-done.19) | copy-start | bytes 24580
  181.4 6.1 %copy-start.3 = (f32[2,1024,2048]{2,1,0:T(8,128)}, f32[2,1024,2048]{2,1,0:T(8,128)S(1)}, u32[]{:S(2)}) copy-start(f32[2,1024,2048]{2,1,0:T(8,128)S(1)} %get-tuple-element.215) | copy-start | bytes 50331652
  181.5 6.1 %copy-start.24 = (bf16[16,2,128]{2,1,0:T(2,128)(2,1)S(1)}, bf16[16,2,128]{2,1,0:T(2,128)(2,1)}, u32[]{:S(2)}) copy-start(bf16[16,2,128]{2,1,0:T(2,128)(2,1)} %reshape_squeeze.7) | copy-start | bytes 24580
  189.7 4.3 copy-start.7
  189.7 4.4 copy-start.9
  213.7 78.8 %all-to-all-start = ((bf16[4,256,256]{1,2,0:T(8,128)(2,1)}), bf16[4,256,256]{1,2,0:T(8,128)(2,1)}, u32[]{:S(2)}, u32[]{:S(2)}) async-start(bf16[4,256,256]{1,2,0:T(8,128)(2,1)} %copy.243), calls=%async_computation | async-start | bytes 1048576 | tf_op jit(solution)/shard_map/all_to_all | solution.py:261
  217.9 167.9 %all-gather.20.cloned.1.call-start = ((), (), s32[]{:S(2)}) async-start(), calls=%async_computation.5 | async-start | bytes 2621440 | tf_op jit(solution)/shard_map/all_gather | solution.py:78
  336.3 3.7 copy-start.26
  340.9 143.6 %all-gather.22.cloned.1.call-start = ((), (), s32[]{:S(2)}) async-start(), calls=%async_computation.6 | async-start | bytes 2621440 | tf_op jit(solution)/shard_map/all_gather | solution.py:78
  395.7 38.3 %copy-start.11 = (f32[256,1024]{1,0:T(8,128)S(1)}, f32[256,1024]{1,0:T(8,128)}, u32[]{:S(2)}) copy-start(f32[256,1024]{1,0:T(8,128)} %copy-done.10) | copy-start | bytes 3145732
  434.0 4.5 copy-start.25
  439.5 3.6 copy-start.2
  (19 other events, 29.3 us)
Sparse Core Ops, SparseCore 0:
  9.6 48.6 all-gather.13
  122.1 22.2 all-gather.23
  146.3 24.1 all-gather.25
  171.9 118.6 all-gather.17
  292.1 44.1 all-gather.15
  341.1 44.6 all-gather.19
  439.6 44.9 all-gather.21
where the time goes:
time: 524 us; the launch traced here: 515 us
  waiting for transfers between devices  237 us (45%)
  blocking collectives  66.2 us (13%)
  other arithmetic  62 us (12%)
  local copies, waits for them, and re-layouts  60.5 us (12%)
  matrix products  59.5 us (11%)
  between operations  16.9 us (3%)
  starting transfers between devices  12 us (2%)
    all_gather x3, waiting for transfers between devices, to_owners(): lax.all_gather(local_rows, 'head', axis=0, tiled=True)  119 us
    all_gather x1, waiting for transfers between devices, local(): lax.all_gather(down_weight + (gathered[0, 1] * 0).astype(down_weight.dtyp...  72.7 us
    all_gather x1, waiting for transfers between devices, local(): lax.all_gather(out_weight + (gathered[0, 0] * 0).astype(out_weight.dtype)...  43.8 us
    all_to_all x1, blocking collectives, local(): hidden_swapped = lax.all_to_all(hidden_pieces, 'head', 0, 0, tiled=False)  38.3 us
    convert_element_type x6, local copies, waits for them, and re-layouts, unit_rows(): widened = values.astype(jnp.float32)  17.8 us
    add x16, other arithmetic, advance(): next_moment = moment_rate[:, None, None] * moment + current_written  16 us
    dot_general x1, matrix products, vocab_maxima(): jnp.dot(piece, vocab_weight, preferred_element_type=jnp.float32)  12.9 us
    dot_general x1, matrix products, local(): jnp.einsum('hqk,khd->qhd', near_weights, all_values, preferred_element_ty...  11.1 us
  transfers between devices with their start and end apart: 10, of which 5 were waited for; matrix products, arithmetic and copies ran while one was open for 16% of the time, Pallas kernels for 0%

commit v1 on v0

--- a/solution.py
+++ b/solution.py
@@ -2,6 +2,7 @@
 import jax.numpy as jnp
 from jax import lax
 from jax.sharding import PartitionSpec as P
+from jax.lax import all_to_all, psum
 
 D = 1024
 HS = 128
@@ -13,6 +14,14 @@
 eps_unit = 1e-06
 score_scale = 10.0
 masked_score = -1e30
+
+
+def time_body(vec, bus_axis):
+    series = []
+    for _ in range(psum(1, axis_name=bus_axis)):
+        series.append(vec)
+    met_up = all_to_all(jnp.stack(series, axis=0), axis_name=bus_axis, split_axis=0, concat_axis=0)
+    return jnp.concatenate(met_up, axis=0)
 
 
 def passed_along(array, axis, by):
@@ -123,9 +132,7 @@
     out_full = lax.all_gather(
         out_weight + (gathered[0, 0] * 0).astype(out_weight.dtype), "head", axis=0, tiled=True
     )
-    down_full = lax.all_gather(
-        down_weight + (gathered[0, 1] * 0).astype(down_weight.dtype), "head", axis=0, tiled=True
-    )
+    down_full = time_body(down_weight + (gathered[0, 1] * 0).astype(down_weight.dtype), "head")
     projected = gathered
     query_unit = unit_rows(projected[:, :current_width].reshape(block_rows, heads_here, HS))
     key_unit = unit_rows(

time: 524 us -> 530 us (1.011)
  waiting for transfers between devices: 237 us -> 248 us
  local copies, waits for them, and re-layouts: 60.5 us -> 52.2 us
    all_to_all x0 -> x1, waiting for transfers between devices: none -> 116 us  [time_body(): all_to_all(jnp.stack(series, axis=0), axis_name=bus_axis, split_axis=0, c...]
    all_gather x1 -> x0, waiting for transfers between devices: 72.7 us -> none  [local(): lax.all_gather(down_weight + (gathered[0, 1] * 0).astype(down_weight.dtyp...]
    all_gather x1, waiting for transfers between devices: 43.8 us -> 0.01 us  [local(): lax.all_gather(out_weight + (gathered[0, 0] * 0).astype(out_weight.dtype)...]
    all_to_all x1, waiting for transfers between devices: 0.01 us -> 12.1 us  [local(): swapped = lax.all_to_all(pieces, 'head', 0, 0, tiled=False)]
    dynamic_update_slice x16, local copies, waits for them, and re-layouts: 8.94 us -> 0.16 us  [local(): lax.scan(advance, (identity_coeffs, zero_state, zero_state), (written, de...]
where the time goes in v1:
time: 530 us; the launch traced here: 520 us
  waiting for transfers between devices  248 us (47%)
  blocking collectives  67 us (13%)
  other arithmetic  59.7 us (11%)
  matrix products  59.4 us (11%)
  local copies, waits for them, and re-layouts  52.2 us (10%)
  between operations  16.9 us (3%)
  starting transfers between devices  16.2 us (3%)
    all_gather x3, waiting for transfers between devices, to_owners(): lax.all_gather(local_rows, 'head', axis=0, tiled=True)  119 us
    all_to_all x1, waiting for transfers between devices, time_body(): all_to_all(jnp.stack(series, axis=0), axis_name=bus_axis, split_axis=0, c...  116 us
    all_to_all x1, blocking collectives, local(): hidden_swapped = lax.all_to_all(hidden_pieces, 'head', 0, 0, tiled=False)  38.3 us
    convert_element_type x6, local copies, waits for them, and re-layouts, unit_rows(): widened = values.astype(jnp.float32)  17.8 us
    add x16, other arithmetic, advance(): next_moment = moment_rate[:, None, None] * moment + current_written  16 us
    dot_general x1, matrix products, vocab_maxima(): jnp.dot(piece, vocab_weight, preferred_element_type=jnp.float32)  12.9 us
    all_to_all x1, waiting for transfers between devices, local(): swapped = lax.all_to_all(pieces, 'head', 0, 0, tiled=False)  12.1 us
    dot_general x1, matrix products, local(): jnp.einsum('hqk,khd->qhd', near_weights, all_values, preferred_element_ty...  11.2 us
  transfers between devices with their start and end apart: 10, of which 5 were waited for; matrix products, arithmetic and copies ran while one was open for 16% of the time, Pallas kernels for 0%

profile of v1, /device:TPU:0, one launch (start us, length us, event | category | flops | bytes accessed | tf_op | source)
XLA Modules:
  0.0 520.3 jit_solution(1867166601838208267)
XLA Ops:
  13.5 44.8 %all-gather.13.cloned.1.call-done = bf16[1024,1024]{1,0:T(8,128)(2,1)} async-done(((bf16[256,1024]{1,0:T(8,128)(2,1)}), bf16[1024,1024]{1,0:T(8,128)(2,1)}) %all-gather.13.cloned.1.call-update) | async-done | bytes 2097168 | tf_op jit(solution)/shard_map/all_gather | solution.py:87
  60.6 3.3 fusion.23
  70.0 2.8 reshape.370
  72.9 3.5 copy.230
  76.5 3.1 convert_multiply_fusion.2
  79.5 3.5 fusion.51
  83.1 29.2 %while.34 = (s32[]{:T(128)}, f32[2,3]{0,1:T(4,128)S(1)}, f32[2,128,128]{2,1,0:T(8,128)S(1)}, f32[2,128,128]{2,1,0:T(8,128)S(1)}, f32[16,2,3]{2,1,0:T(2,128)S(1)}...) while((s32[]{:T(128)}, f32[2,3]{0,1:T(4,128)S(1)}, ...), condition=%wide.region_12.13_spmd.clone, body=%wide.region_11.12_spmd.clone.sunk | while | flops 262167 | bytes 920408 | solution.py:222
  114.6 6.5 %and_and_fusion = pred[1024,2048]{1,0:T(8,128)(4,1)} fusion(s32[2048]{0:T(1024)S(1)} %iota_add_fusion, s32[2048]{0:T(1024)S(1)} %fusion.65, s32[1024]{0:T(1024)S(1)} %iota_add_fusion.1, s32[1024]{0:T(1024)S(1)} %fusion.72, pred[2048]{0:T(1024)(128)(4,1)S(1)} %fusion.69), kind=kLoop, calls=%fused_computation.25 | loop fusion | flops 8388608 | bytes 2123776 | tf_op jit(solution)/shard_map/and | solution.py:156
  121.2 9.8 %all-gather.4 = f32[8,2,3]{2,1,0:T(2,128)} all-gather(f32[1,2,3]{2,1,0:T(2,128)S(1)} %bitcast.141), channel_id=2, replica_groups=mesh['seq'=8,'head'=4] {'seq'}, dimensions={0}, use_global_device_ids=true | all-gather | bytes 216 | tf_op jit(solution)/shard_map/all_gather | solution.py:35
  135.1 3.5 collective-permute-start.1
  138.6 2.8 reshape.369
  144.4 3.6 copy.227
  148.1 3.1 collective-permute-start
  154.6 3.3 stack.4
  157.9 5.3 %all-to-all-start.1 = ((bf16[4,704,1024]{2,1,0:T(8,128)(2,1)}), bf16[4,704,1024]{2,1,0:T(8,128)(2,1)}, u32[]{:S(2)}, u32[]{:S(2)}) async-start(bf16[4,704,1024]{2,1,0:T(8,128)(2,1)} %stack.4), calls=%async_computation.1 | async-start | bytes 11534336 | tf_op jit(solution)/shard_map/all_to_all | solution.py:23
  167.7 3.2 fusion.32
  171.0 4.9 fusion.3
  176.0 5.6 %fusion.4 = f32[2,1024]{1,0:T(2,128)S(1)} fusion(f32[2,1024,2048]{2,1,0:T(8,128)S(1)} %get-tuple-element.215, f32[2,1024]{1,0:T(2,128)S(1)} %max.9, pred[1024,2048]{1,0:T(8,128)(4,1)S(1)} %copy-done.7), kind=kLoop, calls=%fused_computation.24 | loop fusion | flops 20969472 | bytes 18890752 | tf_op jit(solution)/shard_map/reduce_sum | solution.py:172
  183.6 4.3 fusion.29
  192.3 11.2 %fusion.43 = bf16[1024,2,128]{0,2,1:T(8,128)(2,1)} fusion(f32[1024,2,128]{0,2,1:T(8,128)} %copy.243, f32[1024,2,128]{0,2,1:T(8,128)} %convolution_bitcast_fusion, f32[2,1024,2048]{2,1,0:T(8,128)} %copy-done.3, f32[2,1024]{1,0:T(2,128)S(1)} %add.232, f32[2,1024]{1,0:T(2,128)S(1)} %max.9, pred[1024,2048]{1,0:T(8,128)(4,1)} %and_and_fusion, ...), kind=kOutput, calls=%fused_computation.64 | convolution fusion | flops 1101791232 | bytes 22560768 | tf_op jit(solution)/shard_map/hqk,khd->qhd/dot_general | solution.py:175
  207.6 116.1 %all-to-all-done.1 = bf16[4,704,1024]{2,1,0:T(8,128)(2,1)} async-done(((bf16[4,704,1024]{2,1,0:T(8,128)(2,1)}), bf16[4,704,1024]{2,1,0:T(8,128)(2,1)}, u32[]{:S(2)}, u32[]{:S(2)}) %all-to-all-start.1) | async-done | bytes 5767200 | tf_op jit(solution)/shard_map/all_to_all | solution.py:23
  323.8 4.1 all-to-all-start
  329.9 12.1 %all-to-all-done = bf16[4,256,256]{1,2,0:T(8,128)(2,1)} async-done(((bf16[4,256,256]{1,2,0:T(8,128)(2,1)}), bf16[4,256,256]{1,2,0:T(8,128)(2,1)}, u32[]{:S(2)}, u32[]{:S(2)}) %all-to-all-start) | async-done | bytes 524320 | tf_op jit(solution)/shard_map/all_to_all | solution.py:268
  346.7 44.7 %all-gather.17.cloned.1.call-done = bf16[1024,1024]{1,0:T(8,128)(2,1)} async-done(((bf16[256,1024]{1,0:T(8,128)(2,1)}), bf16[1024,1024]{1,0:T(8,128)(2,1)}) %all-gather.17.cloned.1.call-update) | async-done | bytes 2097168 | tf_op jit(solution)/shard_map/all_gather | solution.py:87
  391.4 5.0 fusion.85
  401.4 38.3 %all_to_all.15 = bf16[4,256,704]{1,2,0:T(8,128)(2,1)S(1)} all-to-all(bf16[4,256,704]{1,2,0:T(8,128)(2,1)} %copy.246), channel_id=1, replica_groups=mesh['seq'=8,'head'=4] {'head'}, dimensions={0} | all-to-all | bytes 2883584 | tf_op jit(solution)/shard_map/all_to_all | solution.py:276
  439.7 4.4 multiply_reduce_fusion
  445.5 3.0 slice.102
  451.1 8.8 %all-gather.5 = f32[8,4,2]{1,2,0:T(2,128)S(1)} all-gather(f32[1,4,2]{1,2,0:T(2,128)S(1)} %bitcast.145), channel_id=5, replica_groups=mesh['seq'=8,'head'=4] {'seq'}, dimensions={0}, use_global_device_ids=true | all-gather | bytes 288 | tf_op jit(solution)/shard_map/all_gather | solution.py:286
  460.5 29.7 %all-gather.19.cloned.1.call-done = bf16[1024,1024]{1,0:T(8,128)(2,1)} async-done(((bf16[256,1024]{1,0:T(8,128)(2,1)}), bf16[1024,1024]{1,0:T(8,128)(2,1)}) %all-gather.19.cloned.1.call-update) | async-done | bytes 2097168 | tf_op jit(solution)/shard_map/all_gather | solution.py:87
  490.3 12.9 %convolution_reduce_fusion = f32[1024]{0:T(1024)S(1)} fusion(bf16[1024,1024]{1,0:T(8,128)(2,1)} %all-gather.19.cloned.1.call-done, bf16[1024,4096]{1,0:T(8,128)(2,1)} %param.22), kind=kOutput, calls=%fused_computation.32 | convolution fusion | flops 8594127872 | bytes 10489856 | tf_op jit(solution)/shard_map/dot_general | solution.py:282
  503.2 10.1 %pmax.7 = f32[1024]{0:T(1024)} all-reduce(f32[1024]{0:T(1024)S(1)} %convolution_reduce_fusion), channel_id=1, replica_groups=mesh['seq'=8,'head'=4] {'head'}, use_global_device_ids=true, to_apply=%region_18.19 | all-reduce | flops 1024 | bytes 8192 | tf_op jit(solution)/shard_map/pmax | solution.py:285
  (279 shorter events, 85.5 us)
Async XLA Ops:
  7.2 384.3 %copy-start = (bf16[1024,2,704]{0,2,1:T(8,128)(2,1)S(1)}, bf16[1024,2,704]{0,2,1:T(8,128)(2,1)}, u32[]{:S(2)}) copy-start(bf16[1024,2,704]{0,2,1:T(8,128)(2,1)} %param.20) | copy-start | bytes 8650756
  7.2 3.5 copy-start.22
  7.2 4.6 copy-start.27
  7.2 4.8 copy-start.25
  7.2 4.9 copy-start.26
  7.2 5.6 %copy-start.19 = (f32[3,1024]{1,0:T(4,128)S(1)}, f32[3,1024]{1,0:T(4,128)}, u32[]{:S(2)}) copy-start(f32[3,1024]{1,0:T(4,128)} %param.24) | copy-start | bytes 36868
  7.2 51.1 %all-gather.13.cloned.1.call-start = ((), (), s32[]{:S(2)}) async-start(), calls=%async_computation.3 | async-start | bytes 2621440 | tf_op jit(solution)/shard_map/all_gather | solution.py:87
  8.0 175.0 %all-gather.21.cloned.1.call-start = ((), (), s32[]{:S(2)}) async-start(), calls=%async_computation.7 | async-start | bytes 1179648 | tf_op jit(solution)/shard_map/all_gather | solution.py:35
  12.2 51.7 %copy-start.30 = (s32[16]{0:T(128)}, s32[16]{0:T(128)S(1)}, u32[]{:S(2)}) copy-start(s32[16]{0:T(128)S(1)} %iota_add_fusion.2) | copy-start | bytes 196
  76.4 3.1 copy-start.6
  79.5 3.5 copy-start.29
  83.1 30.0 %copy-start.18 = (bf16[2,16,256]{2,1,0:T(8,128)(2,1)S(1)}, bf16[2,16,256]{2,1,0:T(8,128)(2,1)}, u32[]{:S(2)}) copy-start(bf16[2,16,256]{2,1,0:T(8,128)(2,1)} %param.23) | copy-start | bytes 49156
  113.0 70.0 %all-gather.23.cloned.1.call-start = ((), (), s32[]{:S(2)}) async-start(), calls=%async_computation.8 | async-start | bytes 1179648 | tf_op jit(solution)/shard_map/all_gather | solution.py:35
  121.2 20.2 %copy-start.20 = (f32[2,3]{1,0:T(2,128)}, f32[2,3]{1,0:T(2,128)S(1)}, u32[]{:S(2)}) copy-start(f32[2,3]{1,0:T(2,128)S(1)} %copy.239) | copy-start | bytes 76
  135.1 35.9 %collective-permute-start.1 = (bf16[1024,2,128]{2,0,1:T(8,128)(2,1)S(1)}, bf16[1024,2,128]{2,0,1:T(8,128)(2,1)}, u32[]{:S(2)}, u32[]{:S(2)}) collective-permute-start(bf16[1024,2,128]{2,0,1:T(8,128)(2,1)S(1)} %multiply_convert_fusion.4), channel_id=1, source_target_pairs={{0,4},{4,8},{8,12},{12,16},{16,20},{20,24},{24,28},{1,5},{5,9},{9,... | collective-permute-start | bytes 1572872 | tf_op jit(solution)/shard_map/ppermute | solution.py:30
  148.1 44.2 %collective-permute-start = (bf16[1024,2,128]{0,2,1:T(8,128)(2,1)}, bf16[1024,2,128]{0,2,1:T(8,128)(2,1)}, u32[]{:S(2)}, u32[]{:S(2)}) collective-permute-start(bf16[1024,2,128]{0,2,1:T(8,128)(2,1)} %bitcast.5), channel_id=1, source_target_pairs={{0,4},{4,8},{8,12},{12,16},{16,20},{20,24},{24,28},{1,5},{5,9},{9,... | collective-permute-start | bytes 1572872 | tf_op jit(solution)/shard_map/ppermute | solution.py:30
  157.9 8.0 %copy-start.15 = (bf16[16,2,128]{2,1,0:T(2,128)(2,1)S(1)}, bf16[16,2,128]{2,1,0:T(2,128)(2,1)}, u32[]{:S(2)}) copy-start(bf16[16,2,128]{2,1,0:T(2,128)(2,1)} %reshape_squeeze.6) | copy-start | bytes 24580
  157.9 165.9 %all-to-all-start.1 = ((bf16[4,704,1024]{2,1,0:T(8,128)(2,1)}), bf16[4,704,1024]{2,1,0:T(8,128)(2,1)}, u32[]{:S(2)}, u32[]{:S(2)}) async-start(bf16[4,704,1024]{2,1,0:T(8,128)(2,1)} %stack.4), calls=%async_computation.1 | async-start | bytes 11534336 | tf_op jit(solution)/shard_map/all_to_all | solution.py:23
  163.2 178.7 %all-gather.15.cloned.1.call-start = ((), (), s32[]{:S(2)}) async-start(), calls=%async_computation.4 | async-start | bytes 2621440 | tf_op jit(solution)/shard_map/all_gather | solution.py:132
  165.9 5.1 copy-start.7
  165.9 5.1 copy-start.12
  175.9 5.7 %copy-start.3 = (f32[2,1024,2048]{2,1,0:T(8,128)}, f32[2,1024,2048]{2,1,0:T(8,128)S(1)}, u32[]{:S(2)}) copy-start(f32[2,1024,2048]{2,1,0:T(8,128)S(1)} %get-tuple-element.215) | copy-start | bytes 50331652
  176.0 5.7 %copy-start.14 = (bf16[16,2,128]{2,1,0:T(2,128)(2,1)S(1)}, bf16[16,2,128]{2,1,0:T(2,128)(2,1)}, u32[]{:S(2)}) copy-start(bf16[16,2,128]{2,1,0:T(2,128)(2,1)} %reshape_squeeze.7) | copy-start | bytes 24580
  183.6 4.3 copy-start.9
  183.6 4.3 copy-start.11
  323.8 18.2 %all-to-all-start = ((bf16[4,256,256]{1,2,0:T(8,128)(2,1)}), bf16[4,256,256]{1,2,0:T(8,128)(2,1)}, u32[]{:S(2)}, u32[]{:S(2)}) async-start(bf16[4,256,256]{1,2,0:T(8,128)(2,1)} %copy.244), calls=%async_computation | async-start | bytes 1048576 | tf_op jit(solution)/shard_map/all_to_all | solution.py:268
  327.9 63.5 %all-gather.17.cloned.1.call-start = ((), (), s32[]{:S(2)}) async-start(), calls=%async_computation.5 | async-start | bytes 2621440 | tf_op jit(solution)/shard_map/all_gather | solution.py:87
  342.0 3.7 copy-start.17
  346.7 143.6 %all-gather.19.cloned.1.call-start = ((), (), s32[]{:S(2)}) async-start(), calls=%async_computation.6 | async-start | bytes 2621440 | tf_op jit(solution)/shard_map/all_gather | solution.py:87
  401.4 38.3 %copy-start.5 = (f32[256,1024]{1,0:T(8,128)S(1)}, f32[256,1024]{1,0:T(8,128)}, u32[]{:S(2)}) copy-start(f32[256,1024]{1,0:T(8,128)} %copy-done.4) | copy-start | bytes 3145732
  439.7 4.5 copy-start.16
  445.2 3.6 copy-start.2
  (10 other events, 12.9 us)
Sparse Core Ops, SparseCore 0:
  9.6 48.6 all-gather.12
  113.2 22.1 all-gather.20
  137.3 24.9 all-gather.22
  166.0 83.2 all-gather.14
  346.8 44.5 all-gather.16
  445.3 44.9 all-gather.18
